TPU v7x, 512 devices: a whole 4x8x8 slice. The times are simulated.
512 devices in a mesh: row: 4 (over y_hi), col: 16 (over y_lo, x, core), depth: 8 (over z).
Axes of the slice: x: 4, y: 8 (y_hi: 4, y_lo: 2; y = y_hi * 2 + y_lo), z: 8, core: 2. Of those that a mesh axis runs over, the one named last changes fastest.
Arguments:
- block_values: bfloat16 [32, 16, 16, 128, 128], P(('row', 'depth'), 'col'), may hold values from 0.0049743652 to 0.5
- block_cols: int32 [32, 16, 16], P(('row', 'depth'), 'col'), may hold values from 0 to 511, as said below
- live_count: int32 [32, 16], P(('row', 'depth'), 'col'), may hold values from 8 to 16, as said below
- out_pattern: int32 [4, 16, 32, 2], P('row', 'col'), may hold values from 0 to 511, as said below
Outputs:
- squared_log: bfloat16 [4, 16, 32, 128, 128], P('row', 'col', 'depth')
Inputs may be any that keep to these rules, and one draw needn't show every extreme that they name: Block row i's blocks are its first live_count slots; in every draw some block row is full. `block_cols`: the slots of one block row name distinct block columns. Call (k // 16) % 8 the depth part of a block index k and k // 32 its column group. Among the live slots of one block row at most 2 name a column in any one depth part and at most 2 in any one column group; both bounds are reached in every draw. The 32 entries of out_pattern[r, c] are distinct pairs (i, j) with i // 128 == r and j // 32 == c.
All inputs are finite; a program needn't handle non-finite values.
Results may differ from a plain program's by a relative error of at most 0.001.
Values may be sent and summed in bfloat16 or wider, within the bound.
No kernel may reach another device: no remote copies, remote signals or barrier semaphores. Data moves between devices by JAX's collectives and lax.ppermute only.
A program may use at most 128 MiB of HBM per device.

v0:
```python
import jax
import jax.numpy as jnp
from jax import lax
from jax.sharding import PartitionSpec as P


def pack_slots(values, col_ids, targets, is_live, part_count, capacity):
    row_count = col_ids.shape[0]
    block_size = values.shape[-1]
    chosen = (
        targets[:, :, None] == jnp.arange(part_count, dtype=jnp.int32)[None, None, :]
    ) & is_live[:, :, None]
    running = jnp.cumsum(chosen.astype(jnp.int32), axis=1) - 1
    order_in = jnp.sum(jnp.where(chosen, running, 0), axis=2)
    row_ids = jnp.arange(row_count, dtype=jnp.int32)[:, None]
    total = part_count * row_count * capacity
    position = (targets * row_count + row_ids) * capacity + order_in
    position = jnp.where(is_live, position, total).reshape(-1)
    packed = jnp.zeros((total, block_size, block_size), values.dtype)
    packed = packed.at[position].set(values.reshape(-1, block_size, block_size), mode="drop")
    return packed.reshape(part_count, row_count, capacity, block_size, block_size)


def body(block_values, block_cols, live_count, out_pattern):
    depths = lax.axis_size("depth")
    columns = lax.axis_size("col")
    row_groups = lax.axis_size("row")
    row_index = lax.axis_index("row")
    depth_index = lax.axis_index("depth")
    col_index = lax.axis_index("col")
    slot_count = block_values.shape[2]
    block_size = block_values.shape[3]
    group_rows = columns
    plane_rows = depths * group_rows
    col_block = row_groups * plane_rows // columns
    cap_left = slot_count // depths
    cap_right = 2
    values = block_values.reshape(1, slot_count, block_size, block_size)
    col_ids = block_cols.reshape(1, slot_count)
    counts = live_count.reshape(1)
    slots = jnp.arange(slot_count, dtype=jnp.int32)
    is_live = slots[None, :] < counts[:, None]
    meta = jnp.concatenate([col_ids, counts[:, None]], axis=1).astype(jnp.float32)
    meta = lax.all_gather(meta, ("row", "depth", "col"), axis=0, tiled=True).astype(jnp.int32)
    all_cols = meta[:, :slot_count]
    all_live = slots[None, :] < meta[:, slot_count:]
    left_vals = pack_slots(
        values, col_ids, col_ids // group_rows % depths, is_live, depths, cap_left
    )
    left_vals = lax.all_to_all(left_vals, "depth", split_axis=0, concat_axis=0, tiled=True)
    left_vals = lax.all_gather(left_vals[None], "col", axis=0, tiled=True)
    right_vals = pack_slots(values, col_ids, col_ids // col_block, is_live, columns, cap_right)
    right_vals = lax.all_to_all(right_vals, "col", split_axis=0, concat_axis=0, tiled=True)
    right_parts = [right_vals]
    for shift in range(1, row_groups):
        right_parts.append(
            lax.ppermute(
                right_vals,
                "row",
                perm=[(src, (src + shift) % row_groups) for src in range(row_groups)],
            )
        )
    right_flat = jnp.stack(right_parts).reshape(-1, block_size, block_size)
    pattern_rows = out_pattern[0, 0, :, 0]
    pattern_cols = out_pattern[0, 0, :, 1]
    pattern_len = pattern_rows.shape[0]
    local_row = pattern_rows - row_index * plane_rows
    left_pos = local_row % group_rows * depths + local_row // group_rows
    left_sel = left_pos[:, None] * cap_left + jnp.arange(cap_left, dtype=jnp.int32)[None, :]
    row_cols = jnp.take(all_cols, pattern_rows, axis=0)
    row_live = jnp.take(all_live, pattern_rows, axis=0)
    chosen = row_live & (row_cols // group_rows % depths == depth_index)
    rank = jnp.cumsum(chosen.astype(jnp.int32), axis=1) - 1
    picks = jnp.arange(cap_left, dtype=jnp.int32)
    hit = chosen[:, None, :] & (rank[:, None, :] == picks[None, :, None])
    has_inner = jnp.any(hit, axis=2)
    inner = jnp.sum(jnp.where(hit, row_cols[:, None, :], 0), axis=2)
    inner_cols = jnp.take(all_cols, inner, axis=0)
    inner_live = jnp.take(all_live, inner, axis=0)
    in_group = inner_live & (inner_cols // col_block == col_index)
    before = jnp.cumsum(in_group.astype(jnp.int32), axis=2) - 1
    match = in_group & (inner_cols == pattern_cols[:, None, None])
    found = jnp.any(match, axis=2) & has_inner
    slot = jnp.sum(jnp.where(match, before, 0), axis=2)
    shift_of = (row_index - inner // plane_rows) % row_groups
    right_row = shift_of * columns + inner % group_rows
    left_flat = left_vals.reshape(-1, block_size, block_size)
    left_pick = jnp.take(left_flat, left_sel.reshape(-1), axis=0)
    right_pick = jnp.take(right_flat, (right_row * cap_right + slot).reshape(-1), axis=0)
    right_pick = jnp.where(found.reshape(-1)[:, None, None], right_pick, jnp.zeros_like(right_pick))
    left_pick = left_pick.reshape(pattern_len, cap_left, block_size, block_size)
    right_pick = right_pick.reshape(pattern_len, cap_left, block_size, block_size)
    partial_sum = jnp.einsum(
        "pqab,pqbc->pac", left_pick, right_pick, preferred_element_type=jnp.float32
    )
    share = lax.psum_scatter(partial_sum[None, None], "depth", scatter_dimension=2, tiled=True)
    return jnp.log1p(share).astype(jnp.bfloat16)


def solution(mesh):
    in_specs = (
        P(("row", "depth"), "col", None, None, None),
        P(("row", "depth"), "col", None),
        P(("row", "depth"), "col"),
        P("row", "col", None, None),
    )
    out_specs = P("row", "col", "depth", None, None)
    return jax.shard_map(body, mesh=mesh, in_specs=in_specs, out_specs=out_specs, check_vma=False)
```

profile of v0, /device:TPU:12, one launch (start us, length us, event | category | flops | bytes accessed | tf_op | source)
XLA Modules:
  0.0 870.1 jit_solution(6802126021564995380)
XLA Ops:
  7.2 0.7 and_select_fusion.8
  8.0 0.2 select_reduce_fusion.3
  8.3 0.2 select_reduce_fusion.2
  8.5 0.7 fusion.41
  9.3 2.1 scatter_fusion
  11.3 27.7 %all_to_all.10 = bf16[8,1,2,128,128]{4,3,2,1,0:T(8,128)(2,1)} all-to-all(bf16[8,1,2,128,128]{4,3,2,1,0:T(8,128)(2,1)S(1)} %bitcast.99), channel_id=1, replica_groups=mesh['row'=4,'col'=16,'depth'=8] {'depth'}, dimensions={0} | all-to-all | bytes 1048576 | tf_op jit(solution)/shard_map/all_to_all | solution.py:50
  39.1 1.3 broadcast_in_dim.133
  40.4 2.6 scatter_fusion.1
  43.0 5.7 all-to-all-start.1
  48.9 668.3 %all-gather.1 = f32[512,1,17]{2,1,0:T(1,128)S(1)} all-gather(f32[1,1,17]{2,1,0:T(1,128)S(1)} %fusion.46), channel_id=1, replica_groups=mesh['row'=4,'col'=16,'depth'=8] {'row','depth','col'}, dimensions={0}, use_global_device_ids=true | all-gather | bytes 34884 | tf_op jit(solution)/shard_map/all_gather | solution.py:44
  717.2 0.6 gather_fusion.2
  717.8 0.2 slice_reduce_fusion
  718.0 0.1 iota_compare_fusion
  718.1 0.6 gather_fusion.1
  718.8 0.2 reduce_window_sum.45
  719.1 0.1 select_reduce_fusion.1
  719.4 0.6 gather_fusion.4
  720.0 0.6 gather_fusion.3
  720.8 0.2 fusion.50
  721.0 6.9 collective-permute-start.1
  727.9 1.9 collective-permute-start
  729.8 6.0 collective-permute-start.2
  736.6 0.4 reduce_window_sum.46
  736.9 0.1 select_reduce_fusion
  737.5 15.5 %collective-permute-done.1 = bf16[16,1,2,128,128]{4,3,2,0,1:T(8,128)(2,1)S(1)} collective-permute-done((bf16[16,1,2,128,128]{4,3,2,0,1:T(8,128)(2,1)S(1)}, bf16[16,1,2,128,128]{4,3,2,0,1:T(8,128)(2,1)S(1)}, u32[]{:S(2)}, u32[]{:S(2)}) %collective-permute-start.1) | collective-permute-done | bytes 1048608 | tf_op jit(solution)/shard_map/ppermute | solution.py:57
  753.0 48.9 %collective-permute-done = bf16[16,1,2,128,128]{4,3,2,0,1:T(8,128)(2,1)S(1)} collective-permute-done((bf16[16,1,2,128,128]{4,3,2,0,1:T(8,128)(2,1)S(1)}, bf16[16,1,2,128,128]{4,3,2,0,1:T(8,128)(2,1)S(1)}, u32[]{:S(2)}, u32[]{:S(2)}) %collective-permute-start) | collective-permute-done | bytes 1048608 | tf_op jit(solution)/shard_map/ppermute | solution.py:57
  801.9 3.3 pad_maximum_fusion
  805.2 3.1 gather_fusion.5
  808.3 5.6 gather_fusion
  813.9 3.7 fusion.7
  817.7 43.8 %reduce-scatter.2.cloned.1.call-done = f32[1,1,4,128,128]{4,3,2,1,0:T(8,128)} async-done(((f32[1,1,32,128,128]{4,3,2,1,0:T(8,128)}), f32[1,1,4,128,128]{4,3,2,1,0:T(8,128)}) %reduce-scatter.2.cloned.1.call-update) | async-done | bytes 262160 | tf_op jit(solution)/shard_map/reduce_scatter | solution.py:96
  861.5 1.7 log-plus-one_convert_fusion
  (53 shorter events, 2.1 us)
Async XLA Ops:
  6.5 801.8 %all-gather.4.cloned.1.call-start = ((), (), s32[]{:S(2)}) async-start(), calls=%async_computation.4 | async-start | bytes 8912896 | tf_op jit(solution)/shard_map/all_gather | solution.py:51
  9.3 31.1 %copy-start = (bf16[1,1,16,128,128]{4,3,2,1,0:T(8,128)(2,1)S(1)}, bf16[1,1,16,128,128]{4,3,2,1,0:T(8,128)(2,1)}, u32[]{:S(2)}) copy-start(bf16[1,1,16,128,128]{4,3,2,1,0:T(8,128)(2,1)} %param.4) | copy-start | bytes 1572868
  40.4 8.4 copy-start.1
  40.4 676.7 %copy-start.2 = (s32[1,1,32,2]{2,3,1,0:T(2,128)S(1)}, s32[1,1,32,2]{2,3,1,0:T(2,128)}, u32[]{:S(2)}) copy-start(s32[1,1,32,2]{2,3,1,0:T(2,128)} %param.7) | copy-start | bytes 772
  43.0 678.0 %all-to-all-start.1 = ((bf16[16,1,2,128,128]{4,3,2,1,0:T(8,128)(2,1)}), bf16[16,1,2,128,128]{4,3,2,1,0:T(8,128)(2,1)S(1)}, u32[]{:S(2)}, u32[]{:S(2)}) async-start(bf16[16,1,2,128,128]{4,3,2,1,0:T(8,128)(2,1)} %bitcast.22), calls=%async_computation.1 | async-start | bytes 2097152 | tf_op jit(solution)/shard_map/all_to_all | solution.py:53
  48.7 812.8 %reduce-scatter.2.cloned.1.call-start = ((), (), s32[]{:S(2)}) async-start(), calls=%async_computation.3 | async-start | bytes 2359296 | tf_op jit(solution)/shard_map/reduce_scatter | solution.py:96
  721.0 32.0 %collective-permute-start.1 = (bf16[16,1,2,128,128]{4,3,2,0,1:T(8,128)(2,1)S(1)}, bf16[16,1,2,128,128]{4,3,2,0,1:T(8,128)(2,1)S(1)}, u32[]{:S(2)}, u32[]{:S(2)}) collective-permute-start(bf16[16,1,2,128,128]{4,3,2,0,1:T(8,128)(2,1)S(1)} %bitcast.100), channel_id=1, source_target_pairs={{0,256},{128,384},{256,0},{384,128},{1,257},{129,385},{257,1},{385... | collective-permute-start | bytes 3145736 | tf_op jit(solution)/shard_map/ppermute | solution.py:57
  727.9 74.0 %collective-permute-start = (bf16[16,1,2,128,128]{4,3,2,0,1:T(8,128)(2,1)S(1)}, bf16[16,1,2,128,128]{4,3,2,0,1:T(8,128)(2,1)S(1)}, u32[]{:S(2)}, u32[]{:S(2)}) collective-permute-start(bf16[16,1,2,128,128]{4,3,2,0,1:T(8,128)(2,1)S(1)} %bitcast.101), channel_id=1, source_target_pairs={{0,128},{128,256},{256,384},{384,0},{1,129},{129,257},{257,385},{3... | collective-permute-start | bytes 3145736 | tf_op jit(solution)/shard_map/ppermute | solution.py:57
  729.8 72.1 %collective-permute-start.2 = (bf16[16,1,2,128,128]{4,3,2,1,0:T(8,128)(2,1)S(1)}, bf16[16,1,2,128,128]{4,3,2,1,0:T(8,128)(2,1)}, u32[]{:S(2)}, u32[]{:S(2)}) collective-permute-start(bf16[16,1,2,128,128]{4,3,2,1,0:T(8,128)(2,1)S(1)} %all-to-all-done.1), channel_id=1, source_target_pairs={{0,384},{128,0},{256,128},{384,256},{1,385},{129,1},{257,129},{385... | collective-permute-start | bytes 3145736 | tf_op jit(solution)/shard_map/ppermute | solution.py:57
Sparse Core Ops, SparseCore 0:
  39.2 64.2 all-gather.3
  817.8 43.6 reduce-scatter.1
where the time goes:
time: 871 us; the launch traced here: 870 us
  blocking collectives  696 us (80%)
  waiting for transfers between devices  108 us (12%)
  starting transfers between devices  20.6 us (2%)
  local copies, waits for them, and re-layouts  18.6 us (2%)
  between operations  14.3 us (2%)
    all_gather x1, blocking collectives, body(): lax.all_gather(meta, ('row', 'depth', 'col'), axis=0, tiled=True)  668 us
    ppermute x3, waiting for transfers between devices, body(): lax.ppermute(right_vals, 'row', perm=[(src, (src + shift) % row_groups) f...  64.4 us
    reduce_scatter x1, waiting for transfers between devices, body(): lax.psum_scatter(partial_sum[None, None], 'depth', scatter_dimension=2, t...  43.8 us
    all_to_all x1, blocking collectives, body(): lax.all_to_all(left_vals, 'depth', split_axis=0, concat_axis=0, tiled=True)  27.7 us
  transfers between devices with their start and end apart: 6, of which 3 were waited for; matrix products, arithmetic and copies ran while one was open for 2% of the time, Pallas kernels for 0%

commit v1 on v0

--- a/solution.py
+++ b/solution.py
@@ -41,7 +41,15 @@
     slots = jnp.arange(slot_count, dtype=jnp.int32)
     is_live = slots[None, :] < counts[:, None]
     meta = jnp.concatenate([col_ids, counts[:, None]], axis=1).astype(jnp.float32)
-    meta = lax.all_gather(meta, ("row", "depth", "col"), axis=0, tiled=True).astype(jnp.int32)
+    meta = jnp.concatenate(
+        lax.all_to_all(
+            jnp.stack([meta] * lax.axis_size(("row", "depth", "col"))),
+            ("row", "depth", "col"),
+            0,
+            0,
+        ),
+        axis=0,
+    ).astype(jnp.int32)
     all_cols = meta[:, :slot_count]
     all_live = slots[None, :] < meta[:, slot_count:]
     left_vals = pack_slots(

time: 871 us -> 269 us (0.31)
  the two profiles are of different devices: /device:TPU:12 before, /device:TPU:4 now
where the time goes in v1:
time: 269 us
  waiting for transfers between devices  166 us (62%)
  starting transfers between devices  28.6 us (11%)
  blocking collectives  27.9 us (10%)
  local copies, waits for them, and re-layouts  19.4 us (7%)
  between operations  14.3 us (5%)
  other arithmetic  8.6 us (3%)
  matrix products  3.74 us (1%)
    ppermute x3, waiting for transfers between devices, body(): lax.ppermute(right_vals, 'row', perm=[(src, (src + shift) % row_groups) f...  82.5 us
    reduce_scatter x1, waiting for transfers between devices, body(): lax.psum_scatter(partial_sum[None, None], 'depth', scatter_dimension=2, t...  49.6 us
    all_to_all x1, blocking collectives, body(): lax.all_to_all(left_vals, 'depth', split_axis=0, concat_axis=0, tiled=True)  27.9 us
    all_to_all x1, waiting for transfers between devices, body(): lax.all_to_all(right_vals, 'col', split_axis=0, concat_axis=0, tiled=True)  19.7 us
    all_to_all x1, waiting for transfers between devices, body(): lax.all_to_all(jnp.stack([meta] * lax.axis_size(('row', 'depth', 'col')))...  14.3 us
    all_to_all x1, starting transfers between devices, body(): lax.all_to_all(jnp.stack([meta] * lax.axis_size(('row', 'depth', 'col')))...  12.7 us
    ppermute x3, starting transfers between devices, body(): lax.ppermute(right_vals, 'row', perm=[(src, (src + shift) % row_groups) f...  10.9 us
    gather x1, local copies, waits for them, and re-layouts, body(): left_pick = jnp.take(left_flat, left_sel.reshape(-1), axis=0)  5.59 us
  transfers between devices with their start and end apart: 7, of which 6 were waited for; matrix products, arithmetic and copies ran while one was open for 6% of the time, Pallas kernels for 0%

profile of v1, /device:TPU:4, one launch (start us, length us, event | category | flops | bytes accessed | tf_op | source)
XLA Modules:
  0.0 268.6 jit_solution(8016768821458796365)
XLA Ops:
  7.2 0.7 and_select_fusion.8
  8.0 0.2 select_reduce_fusion.3
  8.3 0.2 select_reduce_fusion.2
  8.5 0.7 fusion.41
  9.3 2.1 scatter_fusion
  11.4 27.9 %all_to_all.15 = bf16[8,1,2,128,128]{4,3,2,1,0:T(8,128)(2,1)} all-to-all(bf16[8,1,2,128,128]{4,3,2,1,0:T(8,128)(2,1)S(1)} %bitcast.86), channel_id=1, replica_groups=mesh['row'=4,'col'=16,'depth'=8] {'depth'}, dimensions={0} | all-to-all | bytes 1048576 | tf_op jit(solution)/shard_map/all_to_all | solution.py:58
  39.3 0.8 stack.12
  40.2 12.7 %all-to-all-start.1 = ((f32[512,1,17]{2,1,0:T(1,128)}), f32[512,1,17]{2,1,0:T(1,128)S(1)}, u32[]{:S(2)}, u32[]{:S(2)}) async-start(f32[512,1,17]{2,1,0:T(1,128)} %stack.12), calls=%async_computation.1 | async-start | bytes 524288 | tf_op jit(solution)/shard_map/all_to_all | solution.py:45
  53.2 1.3 broadcast_in_dim.133
  54.5 2.6 scatter_fusion.1
  57.1 14.3 %all-to-all-done.1 = f32[512,1,17]{2,1,0:T(1,128)S(1)} async-done(((f32[512,1,17]{2,1,0:T(1,128)}), f32[512,1,17]{2,1,0:T(1,128)S(1)}, u32[]{:S(2)}, u32[]{:S(2)}) %all-to-all-start.1) | async-done | bytes 34848 | tf_op jit(solution)/shard_map/all_to_all | solution.py:45
  71.4 4.9 %all-to-all-start.2 = ((bf16[16,1,2,128,128]{4,3,2,1,0:T(8,128)(2,1)}), bf16[16,1,2,128,128]{4,3,2,1,0:T(8,128)(2,1)S(1)}, u32[]{:S(2)}, u32[]{:S(2)}) async-start(bf16[16,1,2,128,128]{4,3,2,1,0:T(8,128)(2,1)} %bitcast.21), calls=%async_computation.2 | async-start | bytes 2097152 | tf_op jit(solution)/shard_map/all_to_all | solution.py:61
  76.5 0.6 gather_fusion.2
  77.1 0.2 slice_reduce_fusion
  77.5 0.6 gather_fusion.1
  78.8 19.7 %all-to-all-done.2 = bf16[16,1,2,128,128]{4,3,2,1,0:T(8,128)(2,1)S(1)} async-done(((bf16[16,1,2,128,128]{4,3,2,1,0:T(8,128)(2,1)}), bf16[16,1,2,128,128]{4,3,2,1,0:T(8,128)(2,1)S(1)}, u32[]{:S(2)}, u32[]{:S(2)}) %all-to-all-start.2) | async-done | bytes 1048608 | tf_op jit(solution)/shard_map/all_to_all | solution.py:61
  98.4 3.0 %collective-permute-start.1 = (bf16[16,1,2,128,128]{4,3,2,0,1:T(8,128)(2,1)S(1)}, bf16[16,1,2,128,128]{4,3,2,0,1:T(8,128)(2,1)S(1)}, u32[]{:S(2)}, u32[]{:S(2)}) collective-permute-start(bf16[16,1,2,128,128]{4,3,2,0,1:T(8,128)(2,1)S(1)} %bitcast.87), channel_id=1, source_target_pairs={{0,256},{128,384},{256,0},{384,128},{1,257},{129,385},{257,1},{385... | collective-permute-start | bytes 3145736 | tf_op jit(solution)/shard_map/ppermute | solution.py:65
  101.4 4.4 %collective-permute-start = (bf16[16,1,2,128,128]{4,3,2,0,1:T(8,128)(2,1)S(1)}, bf16[16,1,2,128,128]{4,3,2,0,1:T(8,128)(2,1)S(1)}, u32[]{:S(2)}, u32[]{:S(2)}) collective-permute-start(bf16[16,1,2,128,128]{4,3,2,0,1:T(8,128)(2,1)S(1)} %bitcast.88), channel_id=1, source_target_pairs={{0,128},{128,256},{256,384},{384,0},{1,129},{129,257},{257,385},{3... | collective-permute-start | bytes 3145736 | tf_op jit(solution)/shard_map/ppermute | solution.py:65
  105.9 3.5 %collective-permute-start.2 = (bf16[16,1,2,128,128]{4,3,2,1,0:T(8,128)(2,1)S(1)}, bf16[16,1,2,128,128]{4,3,2,1,0:T(8,128)(2,1)}, u32[]{:S(2)}, u32[]{:S(2)}) collective-permute-start(bf16[16,1,2,128,128]{4,3,2,1,0:T(8,128)(2,1)S(1)} %all-to-all-done.2), channel_id=1, source_target_pairs={{0,384},{128,0},{256,128},{384,256},{1,385},{129,1},{257,129},{385... | collective-permute-start | bytes 3145736 | tf_op jit(solution)/shard_map/ppermute | solution.py:65
  109.4 0.6 gather_fusion.4
  110.0 0.6 gather_fusion.3
  110.9 0.2 fusion.49
  111.3 0.4 reduce_window_sum.46
  112.2 33.8 %collective-permute-done.1 = bf16[16,1,2,128,128]{4,3,2,0,1:T(8,128)(2,1)S(1)} collective-permute-done((bf16[16,1,2,128,128]{4,3,2,0,1:T(8,128)(2,1)S(1)}, bf16[16,1,2,128,128]{4,3,2,0,1:T(8,128)(2,1)S(1)}, u32[]{:S(2)}, u32[]{:S(2)}) %collective-permute-start.1) | collective-permute-done | bytes 1048608 | tf_op jit(solution)/shard_map/ppermute | solution.py:65
  146.0 27.4 %collective-permute-done = bf16[16,1,2,128,128]{4,3,2,0,1:T(8,128)(2,1)S(1)} collective-permute-done((bf16[16,1,2,128,128]{4,3,2,0,1:T(8,128)(2,1)S(1)}, bf16[16,1,2,128,128]{4,3,2,0,1:T(8,128)(2,1)S(1)}, u32[]{:S(2)}, u32[]{:S(2)}) %collective-permute-start) | collective-permute-done | bytes 1048608 | tf_op jit(solution)/shard_map/ppermute | solution.py:65
  173.4 21.3 %collective-permute-done.2 = bf16[16,1,2,128,128]{4,3,2,1,0:T(8,128)(2,1)} collective-permute-done((bf16[16,1,2,128,128]{4,3,2,1,0:T(8,128)(2,1)S(1)}, bf16[16,1,2,128,128]{4,3,2,1,0:T(8,128)(2,1)}, u32[]{:S(2)}, u32[]{:S(2)}) %collective-permute-start.2) | collective-permute-done | bytes 1048608 | tf_op jit(solution)/shard_map/ppermute | solution.py:65
  194.7 3.3 %pad_maximum_fusion = bf16[4,16,1,2,128,128]{5,4,3,1,2,0:T(8,128)(2,1)} fusion(bf16[1,16,1,2,128,128]{5,4,3,1,2,0:T(8,128)(2,1)} %bitcast.27, bf16[1,16,1,2,128,128]{5,4,3,1,2,0:T(8,128)(2,1)S(1)} %bitcast.97, bf16[1,16,1,2,128,128]{5,4,3,1,2,0:T(8,128)(2,1)S(1)} %bitcast.98, bf16[1,16,1,2,128,128]{5,4,3,1,2,0:T(8,128)(2,1)S(1)} %bitcast.89), kind=kLoop, calls=%fused_computation.8 | loop fusion | flops 6291456 | bytes 8388608 | tf_op jit(solution)/shard_map/stack | solution.py:71
  198.0 3.1 %gather_fusion.5 = bf16[64,128,128]{2,1,0:T(8,128)(2,1)S(1)} fusion(bf16[128,128,128]{2,1,0:T(8,128)(2,1)} %bitcast.85, s32[1024]{0:T(1024)S(1)} %pad_clamp_fusion), kind=kCustom, calls=%fused_computation.5 | custom fusion | bytes 4194560 | tf_op jit(solution)/shard_map/jit(_take)/gather | solution.py:97
  201.2 5.6 %gather_fusion = bf16[64,128,128]{2,1,0:T(8,128)(2,1)} fusion(bf16[256,128,128]{2,1,0:T(8,128)(2,1)} %bitcast.99, s32[1024]{0:T(1024)S(1)} %pad_clamp_fusion.3), kind=kCustom, calls=%fused_computation | custom fusion | bytes 4194560 | tf_op jit(solution)/shard_map/jit(_take)/gather | solution.py:96
  206.8 3.7 %fusion.7 = f32[1,1,32,128,128]{4,3,2,1,0:T(8,128)} fusion(bf16[32,2,128,128]{3,2,1,0:T(8,128)(2,1)S(1)} %bitcast.92, pred[32,2]{1,0:T(8,128)(4,1)S(1)} %copy.20, pred[32,2]{1,0:T(8,128)(4,1)S(1)} %copy.19, bf16[32,2,128,128]{3,2,1,0:T(8,128)(2,1)} %bitcast.93, pred[32,2]{1,0:T(8,128)(4,1)S(1)} %copy.13), kind=kOutput, calls=%fused_computation.16 | convolution fusion | flops 271581184 | bytes 6291648 | tf_op jit(solution)/shard_map/pqab,pqbc->pac/dot_general | solution.py:101
  210.5 49.6 %reduce-scatter.2.cloned.1.call-done = f32[1,1,4,128,128]{4,3,2,1,0:T(8,128)} async-done(((f32[1,1,32,128,128]{4,3,2,1,0:T(8,128)}), f32[1,1,4,128,128]{4,3,2,1,0:T(8,128)}) %reduce-scatter.2.cloned.1.call-update) | async-done | bytes 262160 | tf_op jit(solution)/shard_map/reduce_scatter | solution.py:104
  260.1 1.7 log-plus-one_convert_fusion
  (55 shorter events, 2.6 us)
Async XLA Ops:
  6.5 32.7 %copy-start.1 = (s32[1,1,16]{2,1,0:T(1,128)S(1)}, s32[1,1,16]{2,1,0:T(1,128)}, u32[]{:S(2)}) copy-start(s32[1,1,16]{2,1,0:T(1,128)} %param.5) | copy-start | bytes 196
  6.5 194.6 %all-gather.3.cloned.1.call-start = ((), (), s32[]{:S(2)}) async-start(), calls=%async_computation.5 | async-start | bytes 8912896 | tf_op jit(solution)/shard_map/all_gather | solution.py:59
  9.3 43.6 %copy-start.2 = (s32[1,1,32,2]{2,3,1,0:T(2,128)S(1)}, s32[1,1,32,2]{2,3,1,0:T(2,128)}, u32[]{:S(2)}) copy-start(s32[1,1,32,2]{2,3,1,0:T(2,128)} %param.7) | copy-start | bytes 772
  11.4 43.1 %copy-start = (bf16[1,1,16,128,128]{4,3,2,1,0:T(8,128)(2,1)S(1)}, bf16[1,1,16,128,128]{4,3,2,1,0:T(8,128)(2,1)}, u32[]{:S(2)}) copy-start(bf16[1,1,16,128,128]{4,3,2,1,0:T(8,128)(2,1)} %param.4) | copy-start | bytes 1572868
  40.2 31.2 %all-to-all-start.1 = ((f32[512,1,17]{2,1,0:T(1,128)}), f32[512,1,17]{2,1,0:T(1,128)S(1)}, u32[]{:S(2)}, u32[]{:S(2)}) async-start(f32[512,1,17]{2,1,0:T(1,128)} %stack.12), calls=%async_computation.1 | async-start | bytes 524288 | tf_op jit(solution)/shard_map/all_to_all | solution.py:45
  71.4 27.0 %all-to-all-start.2 = ((bf16[16,1,2,128,128]{4,3,2,1,0:T(8,128)(2,1)}), bf16[16,1,2,128,128]{4,3,2,1,0:T(8,128)(2,1)S(1)}, u32[]{:S(2)}, u32[]{:S(2)}) async-start(bf16[16,1,2,128,128]{4,3,2,1,0:T(8,128)(2,1)} %bitcast.21), calls=%async_computation.2 | async-start | bytes 2097152 | tf_op jit(solution)/shard_map/all_to_all | solution.py:61
  76.3 183.8 %reduce-scatter.2.cloned.1.call-start = ((), (), s32[]{:S(2)}) async-start(), calls=%async_computation.4 | async-start | bytes 2359296 | tf_op jit(solution)/shard_map/reduce_scatter | solution.py:104
  98.4 47.6 %collective-permute-start.1 = (bf16[16,1,2,128,128]{4,3,2,0,1:T(8,128)(2,1)S(1)}, bf16[16,1,2,128,128]{4,3,2,0,1:T(8,128)(2,1)S(1)}, u32[]{:S(2)}, u32[]{:S(2)}) collective-permute-start(bf16[16,1,2,128,128]{4,3,2,0,1:T(8,128)(2,1)S(1)} %bitcast.87), channel_id=1, source_target_pairs={{0,256},{128,384},{256,0},{384,128},{1,257},{129,385},{257,1},{385... | collective-permute-start | bytes 3145736 | tf_op jit(solution)/shard_map/ppermute | solution.py:65
  101.4 72.0 %collective-permute-start = (bf16[16,1,2,128,128]{4,3,2,0,1:T(8,128)(2,1)S(1)}, bf16[16,1,2,128,128]{4,3,2,0,1:T(8,128)(2,1)S(1)}, u32[]{:S(2)}, u32[]{:S(2)}) collective-permute-start(bf16[16,1,2,128,128]{4,3,2,0,1:T(8,128)(2,1)S(1)} %bitcast.88), channel_id=1, source_target_pairs={{0,128},{128,256},{256,384},{384,0},{1,129},{129,257},{257,385},{3... | collective-permute-start | bytes 3145736 | tf_op jit(solution)/shard_map/ppermute | solution.py:65
  105.9 88.8 %collective-permute-start.2 = (bf16[16,1,2,128,128]{4,3,2,1,0:T(8,128)(2,1)S(1)}, bf16[16,1,2,128,128]{4,3,2,1,0:T(8,128)(2,1)}, u32[]{:S(2)}, u32[]{:S(2)}) collective-permute-start(bf16[16,1,2,128,128]{4,3,2,1,0:T(8,128)(2,1)S(1)} %all-to-all-done.2), channel_id=1, source_target_pairs={{0,384},{128,0},{256,128},{384,256},{1,385},{129,1},{257,129},{385... | collective-permute-start | bytes 3145736 | tf_op jit(solution)/shard_map/ppermute | solution.py:65
Sparse Core Ops, SparseCore 0:
  39.4 69.3 all-gather.2
  210.6 49.3 reduce-scatter.1
